TPU v7x, 256 devices: a whole 4x4x8 slice. The times are simulated.
256 devices in a mesh: heads: 32 (over z_hi, y, x), width: 8 (over z_lo, core).
Axes of the slice: x: 4, y: 4, z: 8 (z_hi: 2, z_lo: 4; z = z_hi * 4 + z_lo), core: 2. Of those that a mesh axis runs over, the one named last changes fastest.
Arguments:
- states: bfloat16 [1536, 6144], P('heads', 'width'), may hold values from -6 to 6
- segment_ids: int32 [1536], replicated, may hold values from 0 to 11, never falling along the last dimension, each value on 1 to 1344 neighbouring positions
- attn_gain: float32 [6144], P('width'), may hold values from 0.1 to 1.9
- attn_shift: float32 [6144], P('width'), may hold values from -3 to 3
- mlp_gain: float32 [6144], P('width'), may hold values from 0.1 to 1.9
- mlp_shift: float32 [6144], P('width'), may hold values from -3 to 3
- qkv_weight: bfloat16 [6144, 18432], P('width', 'heads'), may hold values from -0.078125 to 0.078125
- qkv_bias: float32 [18432], P('heads'), may hold values from -6 to 6
- dense_weight: bfloat16 [6144, 6144], P('heads', 'width'), may hold values from -0.078125 to 0.078125
- dense_bias: float32 [6144], P('width'), may hold values from -2 to 2
- up_weight: bfloat16 [6144, 24576], P('width', 'heads'), may hold values from -0.078125 to 0.078125
- up_bias: float32 [24576], P('heads'), may hold values from -3 to 3
- down_weight: bfloat16 [24576, 6144], P('heads', 'width'), may hold values from -0.0390625 to 0.0390625
- down_bias: float32 [6144], P('width'), may hold values from -2 to 2
Outputs:
- layer_out: bfloat16 [1536, 6144], P('heads', 'width')
- key_cache: bfloat16 [1536, 6144], P('width', 'heads')
- value_cache: bfloat16 [1536, 6144], P('width', 'heads')
Inputs may be any that keep to these rules, and one draw needn't show every extreme that they name: `segment_ids`: document numbers never fall along the tokens; each document has 1 to 1344 tokens and one has exactly 1344.
All inputs are finite; a program needn't handle non-finite values.
Results may differ from a plain program's by a relative error of at most 0.017.
Values may be sent and summed in bfloat16 or wider, within the bound.
No kernel may reach another device: no remote copies, remote signals or barrier semaphores. Data moves between devices by JAX's collectives and lax.ppermute only.
A program may use at most 64 MiB of HBM per device.

v0:
```python
import jax
import jax.numpy as jnp
from jax import lax
from jax.sharding import PartitionSpec as P

HD = 96
ROT = 24
D = 6144
norm_epsilon = 1e-05


def positions_of(segments):
    count = segments.shape[0]
    row_index = jnp.arange(count, dtype=jnp.int32)
    change = jnp.concatenate([jnp.ones((1,), bool), segments[1:] != segments[:-1]])
    first = lax.cummax(jnp.where(change, row_index, 0), axis=0)
    return (row_index - first).astype(jnp.float32)


def rotary(values, positions):
    half_rot = ROT // 2
    inverse = 10000.0 ** (-(jnp.arange(half_rot, dtype=jnp.float32) * 2.0 / ROT))
    angles = positions[:, None] * inverse[None, :]
    cosine = jnp.cos(angles)[:, None, :]
    sine_part = jnp.sin(angles)[:, None, :]
    first_half = values[..., :half_rot]
    second_half = values[..., half_rot:ROT]
    return jnp.concatenate(
        [
            first_half * cosine - second_half * sine_part,
            second_half * cosine + first_half * sine_part,
            values[..., ROT:],
        ],
        axis=-1,
    )


def on_device(
    states,
    segment_ids,
    attn_gain,
    attn_shift,
    mlp_gain,
    mlp_shift,
    qkv_weight,
    qkv_bias,
    dense_weight,
    dense_bias,
    up_weight,
    up_bias,
    down_weight,
    down_bias,
):
    floats = states.astype(jnp.float32)
    row_sums, square_sums = lax.psum((jnp.sum(floats, -1), jnp.sum(floats * floats, -1)), "width")
    row_mean = (row_sums / D)[:, None]
    row_var = (square_sums / D)[:, None] - row_mean * row_mean
    normed = ((floats - row_mean) * lax.rsqrt(row_var + norm_epsilon)).astype(jnp.bfloat16)
    qkv_cols = qkv_weight.shape[1]
    heads_dev = qkv_cols // (3 * HD)
    block_f = lax.all_gather(normed, "heads", axis=0, tiled=True).astype(jnp.float32)
    attn_in = (block_f * attn_gain + attn_shift).astype(jnp.bfloat16)
    mlp_in = (block_f * mlp_gain + mlp_shift).astype(jnp.bfloat16)
    projected = jnp.concatenate(
        [
            jnp.dot(attn_in, qkv_weight, preferred_element_type=jnp.float32),
            jnp.dot(mlp_in, up_weight, preferred_element_type=jnp.float32),
        ],
        axis=1,
    )
    qkv_part = projected[:, :qkv_cols]
    up_part = projected[:, qkv_cols:]
    all_tokens = projected.shape[0]
    own_rows = all_tokens // lax.axis_size("width")
    row_zero = lax.axis_index("width") * own_rows
    positions = positions_of(segment_ids)
    own_segments = lax.dynamic_slice_in_dim(segment_ids, row_zero, own_rows)
    own_index = row_zero + jnp.arange(own_rows, dtype=jnp.int32)
    score_scale = 1.0 / HD**0.5
    own_positions = lax.dynamic_slice_in_dim(positions, row_zero, own_rows)
    qkv_own, up_own = (
        lax.psum_scatter(qkv_part, "width", scatter_dimension=0, tiled=True),
        lax.psum_scatter(up_part, "width", scatter_dimension=0, tiled=True),
    )
    shaped = (qkv_own + qkv_bias).reshape(qkv_own.shape[0], heads_dev, 3, HD)
    queries = rotary(shaped[:, :, 0, :], own_positions).astype(jnp.bfloat16)
    keys_part = rotary(shaped[:, :, 1, :], own_positions).astype(jnp.bfloat16)
    values_part = shaped[:, :, 2, :].astype(jnp.bfloat16)
    width_cols = heads_dev * HD
    key_cache = keys_part.reshape(-1, width_cols)
    value_cache = values_part.reshape(-1, width_cols)
    run_max = jnp.full((heads_dev, own_rows), -1e30, jnp.float32)
    key_rows = lax.all_gather(key_cache, "width", axis=0, tiled=True)
    value_rows = lax.all_gather(value_cache, "width", axis=0, tiled=True)
    count = key_rows.shape[0]
    key_heads = key_rows.reshape(count, heads_dev, HD)
    value_heads = value_rows.reshape(count, heads_dev, HD)
    scores = (
        jnp.einsum("rhd,nhd->hrn", queries, key_heads, preferred_element_type=jnp.float32)
        * score_scale
    )
    key_index = jnp.arange(count, dtype=jnp.int32)
    allowed = (own_segments[:, None] == segment_ids[None, :]) & (
        key_index[None, :] <= own_index[:, None]
    )
    scores = jnp.where(allowed[None], scores, -1e30)
    new_max = jnp.maximum(run_max, jnp.max(scores, -1))
    weights = jnp.where(allowed[None], jnp.exp(scores - new_max[..., None]), 0.0)
    new_sum = jnp.sum(weights, -1)
    mixed = jnp.einsum(
        "hrn,nhd->hrd",
        weights.astype(jnp.bfloat16),
        value_heads,
        preferred_element_type=jnp.float32,
    )
    attended = (
        (mixed / new_sum[..., None])
        .transpose(1, 0, 2)
        .reshape(own_rows, heads_dev * HD)
        .astype(jnp.bfloat16)
    )
    attn_part = jnp.dot(
        lax.all_gather(attended, "width", axis=0, tiled=True),
        dense_weight,
        preferred_element_type=jnp.float32,
    )
    hidden = jax.nn.gelu(up_own + up_bias, approximate=False).astype(jnp.bfloat16)
    mlp_part = jnp.dot(
        lax.all_gather(hidden, "width", axis=0, tiled=True),
        down_weight,
        preferred_element_type=jnp.float32,
    )
    summed = lax.psum_scatter(
        attn_part.astype(jnp.bfloat16), "heads", scatter_dimension=0, tiled=True
    ).astype(jnp.float32) + lax.psum_scatter(
        mlp_part.astype(jnp.bfloat16), "heads", scatter_dimension=0, tiled=True
    ).astype(
        jnp.float32
    )
    layer_out = (floats + summed + dense_bias + down_bias).astype(jnp.bfloat16)
    return (layer_out, key_cache, value_cache)


def solution(mesh):
    in_specs = (
        P("heads", "width"),
        P(),
        P("width"),
        P("width"),
        P("width"),
        P("width"),
        P("width", "heads"),
        P("heads"),
        P("heads", "width"),
        P("width"),
        P("width", "heads"),
        P("heads"),
        P("heads", "width"),
        P("width"),
    )
    out_specs = (P("heads", "width"), P("width", "heads"), P("width", "heads"))
    return jax.shard_map(
        on_device, mesh=mesh, in_specs=in_specs, out_specs=out_specs, check_vma=False
    )
```

profile of v0, /device:TPU:2, one launch (start us, length us, event | category | flops | bytes accessed | tf_op | source)
XLA Modules:
  0.0 825.1 jit_solution(1113341373791377234)
XLA Ops:
  7.2 1.1 convert_reduce_fusion
  8.3 17.6 %all-reduce = (f32[48]{0:T(128)S(1)}, f32[48]{0:T(128)S(1)}) all-reduce(f32[48]{0:T(128)S(1)} %get-tuple-element.13, f32[48]{0:T(128)S(1)} %get-tuple-element.12), channel_id=1, replica_groups=mesh['heads'=32,'width'=8] {'width'}, use_global_device_ids=true, to_apply=%region_3.0 | all-reduce | flops 96 | bytes 768 | tf_op jit(solution)/shard_map/psum | solution.py:55
  26.0 1.6 fusion.41
  27.7 92.7 %all-gather.3.cloned.1.call-done = bf16[1536,768]{1,0:T(8,128)(2,1)} async-done(((bf16[48,768]{1,0:T(8,128)(2,1)}), bf16[1536,768]{1,0:T(8,128)(2,1)}) %all-gather.3.cloned.1.call-update) | async-done | bytes 2359312 | tf_op jit(solution)/shard_map/all_gather | solution.py:61
  120.4 5.8 fusion.5
  126.3 1.6 copy-done.10
  127.9 5.1 fusion.7
  133.1 0.6 copy-done.5
  134.0 0.3 reduce-window.9
  134.5 47.2 %reduce-scatter.9.cloned.1.call-done = f32[192,768]{1,0:T(8,128)} async-done(((f32[1536,768]{1,0:T(8,128)}), f32[192,768]{1,0:T(8,128)}) %reduce-scatter.9.cloned.1.call-update) | async-done | bytes 589840 | tf_op jit(solution)/shard_map/reduce_scatter | solution.py:83
  181.7 3.1 fusion.32
  185.0 0.1 multiply_cosine_fusion
  185.4 0.5 fusion.19
  185.8 49.9 %reduce-scatter.5.cloned.1.call-done = f32[192,576]{1,0:T(8,128)} async-done(((f32[1536,576]{1,0:T(8,128)}), f32[192,576]{1,0:T(8,128)}) %reduce-scatter.5.cloned.1.call-update) | async-done | bytes 442384 | tf_op jit(solution)/shard_map/reduce_scatter | solution.py:82
  235.8 1.1 broadcast_add_fusion
  236.8 0.2 copy.38
  237.3 0.8 copy.46
  238.3 0.8 subtract_convert_fusion.1
  239.5 17.0 %all_gather.16 = bf16[1536,192]{1,0:T(8,128)(2,1)S(1)} all-gather(bf16[192,192]{1,0:T(8,128)(2,1)S(1)} %copy.44), channel_id=1, replica_groups=mesh['heads'=32,'width'=8] {'width'}, dimensions={0}, use_global_device_ids=true | all-gather | bytes 663552 | tf_op jit(solution)/shard_map/all_gather | solution.py:93
  256.6 0.3 copy.45
  256.9 18.8 %all_gather.17 = bf16[1536,192]{1,0:T(8,128)(2,1)S(1)} all-gather(bf16[192,192]{1,0:T(8,128)(2,1)S(1)} %copy-done.2), channel_id=1, replica_groups=mesh['heads'=32,'width'=8] {'width'}, dimensions={0}, use_global_device_ids=true | all-gather | bytes 663552 | tf_op jit(solution)/shard_map/all_gather | solution.py:94
  275.7 0.3 copy.47
  275.9 1.7 fusion.55
  277.7 0.7 fusion.13
  278.4 0.7 fusion.27
  279.2 15.8 %all_gather.18 = bf16[1536,192]{1,0:T(8,128)(2,1)S(1)} all-gather(bf16[192,192]{1,0:T(8,128)(2,1)S(1)} %copy.48), channel_id=1, replica_groups=mesh['heads'=32,'width'=8] {'width'}, dimensions={0}, use_global_device_ids=true | all-gather | bytes 663552 | tf_op jit(solution)/shard_map/all_gather | solution.py:123
  295.0 2.2 convolution_convert_fusion.1
  297.3 1.2 copy-done.11
  298.5 5.1 convolution_convert_fusion
  303.6 252.6 %reduce-scatter.7.cloned.1.call-done = bf16[48,768]{1,0:T(8,128)(2,1)} async-done(((bf16[1536,768]{1,0:T(8,128)(2,1)}), bf16[48,768]{1,0:T(8,128)(2,1)}) %reduce-scatter.7.cloned.1.call-update) | async-done | bytes 73744 | tf_op jit(solution)/shard_map/reduce_scatter | solution.py:133
  556.2 260.5 %reduce-scatter.11.cloned.1.call-done = bf16[48,768]{1,0:T(8,128)(2,1)} async-done(((bf16[1536,768]{1,0:T(8,128)(2,1)}), bf16[48,768]{1,0:T(8,128)(2,1)}) %reduce-scatter.11.cloned.1.call-update) | async-done | bytes 73744 | tf_op jit(solution)/shard_map/reduce_scatter | solution.py:135
  816.7 1.6 fusion.45
  (62 shorter events, 2.2 us)
Async XLA Ops:
  7.2 113.2 %copy-start = (bf16[768,768]{1,0:T(8,128)(2,1)S(1)}, bf16[768,768]{1,0:T(8,128)(2,1)}, u32[]{:S(2)}) copy-start(bf16[768,768]{1,0:T(8,128)(2,1)} %param.24) | copy-start | bytes 3538948
  7.2 113.2 %all-gather.3.cloned.1.call-start = ((), (), s32[]{:S(2)}) async-start(), calls=%async_computation.4 | async-start | bytes 2433024 | tf_op jit(solution)/shard_map/all_gather | solution.py:61
  27.6 154.1 %reduce-scatter.9.cloned.1.call-start = ((), (), s32[]{:S(2)}) async-start(), calls=%async_computation.7 | async-start | bytes 5308416 | tf_op jit(solution)/shard_map/reduce_scatter | solution.py:83
  126.2 1.7 copy-start.10
  126.2 1.7 copy-start.12
  126.2 1.7 copy-start.13
  126.3 109.5 %reduce-scatter.5.cloned.1.call-start = ((), (), s32[]{:S(2)}) async-start(), calls=%async_computation.5 | async-start | bytes 4423680 | tf_op jit(solution)/shard_map/reduce_scatter | solution.py:82
  133.0 0.7 copy-start.5
  133.0 48.7 %copy-start.6 = (f32[768]{0:T(1024)S(1)}, f32[768]{0:T(1024)}, u32[]{:S(2)}) copy-start(f32[768]{0:T(1024)} %param.25) | copy-start | bytes 9220
  133.0 102.8 %copy-start.7 = (f32[576]{0:T(1024)S(1)}, f32[576]{0:T(1024)}, u32[]{:S(2)}) copy-start(f32[576]{0:T(1024)} %param.21) | copy-start | bytes 6916
  133.1 164.2 %all-gather.5.cloned.1.call-start = ((), (), s32[]{:S(2)}) async-start(), calls=%async_computation.8 | async-start | bytes 2654208 | tf_op jit(solution)/shard_map/all_gather | solution.py:129
  184.8 371.4 %reduce-scatter.7.cloned.1.call-start = ((), (), s32[]{:S(2)}) async-start(), calls=%async_computation.6 | async-start | bytes 2433024 | tf_op jit(solution)/shard_map/reduce_scatter | solution.py:133
  238.2 18.6 %copy-start.2 = (bf16[192,192]{1,0:T(8,128)(2,1)S(1)}, bf16[192,192]{1,0:T(8,128)(2,1)}, u32[]{:S(2)}) copy-start(bf16[192,192]{1,0:T(8,128)(2,1)} %copy.46) | copy-start | bytes 221188
  239.5 17.3 %copy-start.3 = (bf16[192,192]{1,0:T(8,128)(2,1)}, bf16[192,192]{1,0:T(8,128)(2,1)S(1)}, u32[]{:S(2)}) copy-start(bf16[192,192]{1,0:T(8,128)(2,1)S(1)} %copy.44) | copy-start | bytes 221188
  278.4 16.6 %copy-start.4 = (bf16[192,768]{1,0:T(8,128)(2,1)S(1)}, bf16[192,768]{1,0:T(8,128)(2,1)}, u32[]{:S(2)}) copy-start(bf16[192,768]{1,0:T(8,128)(2,1)} %param.22) | copy-start | bytes 884740
  297.2 1.3 copy-start.11
  297.2 519.4 %reduce-scatter.11.cloned.1.call-start = ((), (), s32[]{:S(2)}) async-start(), calls=%async_computation.9 | async-start | bytes 2433024 | tf_op jit(solution)/shard_map/reduce_scatter | solution.py:135
  303.6 513.1 %copy-start.1 = (bf16[48,768]{1,0:T(8,128)(2,1)S(1)}, bf16[48,768]{1,0:T(8,128)(2,1)}, u32[]{:S(2)}) copy-start(bf16[48,768]{1,0:T(8,128)(2,1)} %param.14) | copy-start | bytes 221188
  303.6 513.1 %copy-start.8 = (f32[768]{0:T(1024)S(1)}, f32[768]{0:T(1024)}, u32[]{:S(2)}) copy-start(f32[768]{0:T(1024)} %param.27) | copy-start | bytes 9220
  303.6 513.1 %copy-start.9 = (f32[768]{0:T(1024)S(1)}, f32[768]{0:T(1024)}, u32[]{:S(2)}) copy-start(f32[768]{0:T(1024)} %param.23) | copy-start | bytes 9220
Sparse Core Ops, SparseCore 0:
  27.7 92.6 all-gather.2
  126.4 55.2 reduce-scatter.8
  184.3 51.4 reduce-scatter.4
  237.4 44.4 all-gather.4
  297.4 258.7 reduce-scatter.6
  561.4 255.1 reduce-scatter.10
where the time goes:
time: 826 us; the launch traced here: 825 us
  waiting for transfers between devices  703 us (85%)
  blocking collectives  69.3 us (8%)
  matrix products  20.7 us (3%)
  between operations  14.3 us (2%)
  other arithmetic  11.4 us (1%)
    reduce_scatter x1, waiting for transfers between devices, on_device(): lax.psum_scatter(mlp_part.astype(jnp.bfloat16), 'heads', scatter_dimensio...  260 us
    reduce_scatter x1, waiting for transfers between devices, on_device(): lax.psum_scatter(attn_part.astype(jnp.bfloat16), 'heads', scatter_dimensi...  253 us
    all_gather x1, waiting for transfers between devices, on_device(): lax.all_gather(normed, 'heads', axis=0, tiled=True).astype(jnp.float32)  92.7 us
    reduce_scatter x1, waiting for transfers between devices, on_device(): lax.psum_scatter(qkv_part, 'width', scatter_dimension=0, tiled=True)  49.9 us
    reduce_scatter x1, waiting for transfers between devices, on_device(): lax.psum_scatter(up_part, 'width', scatter_dimension=0, tiled=True)  47.2 us
    all_gather x1, blocking collectives, on_device(): value_rows = lax.all_gather(value_cache, 'width', axis=0, tiled=True)  18.8 us
    psum x1, blocking collectives, on_device(): lax.psum((jnp.sum(floats, -1), jnp.sum(floats * floats, -1)), 'width')  17.6 us
    all_gather x1, blocking collectives, on_device(): key_rows = lax.all_gather(key_cache, 'width', axis=0, tiled=True)  17 us
  transfers between devices with their start and end apart: 6, of which 5 were waited for; matrix products, arithmetic and copies ran while one was open for 3% of the time, Pallas kernels for 0%

commit v1 on v0

--- a/solution.py
+++ b/solution.py
@@ -58,7 +58,9 @@
     normed = ((floats - row_mean) * lax.rsqrt(row_var + norm_epsilon)).astype(jnp.bfloat16)
     qkv_cols = qkv_weight.shape[1]
     heads_dev = qkv_cols // (3 * HD)
-    block_f = lax.all_gather(normed, "heads", axis=0, tiled=True).astype(jnp.float32)
+    block_f = jnp.concatenate(
+        lax.all_to_all(jnp.stack([normed] * lax.axis_size("heads")), "heads", 0, 0), axis=0
+    ).astype(jnp.float32)
     attn_in = (block_f * attn_gain + attn_shift).astype(jnp.bfloat16)
     mlp_in = (block_f * mlp_gain + mlp_shift).astype(jnp.bfloat16)
     projected = jnp.concatenate(

time: 826 us -> 798 us (0.966)
  waiting for transfers between devices: 703 us -> 614 us
  blocking collectives: 69.3 us -> 134 us
    all_gather x1 -> x0, waiting for transfers between devices: 92.7 us -> none  [on_device(): lax.all_gather(normed, 'heads', axis=0, tiled=True).astype(jnp.float32)]
    all_to_all x0 -> x1, blocking collectives: none -> 64.9 us  [on_device(): lax.all_to_all(jnp.stack([normed] * lax.axis_size('heads')), 'heads', 0, 0)]
  transfers between devices with their start and end apart: 6 -> 5, of which waited for: 5 -> 4; matrix products, arithmetic and copies ran while one was open for 3% -> 3% of each run, Pallas kernels for 0% -> 0%
where the time goes in v1:
time: 798 us
  waiting for transfers between devices  614 us (77%)
  blocking collectives  134 us (17%)
  matrix products  19 us (2%)
  between operations  14 us (2%)
  other arithmetic  10.7 us (1%)
    reduce_scatter x1, waiting for transfers between devices, on_device(): lax.psum_scatter(mlp_part.astype(jnp.bfloat16), 'heads', scatter_dimensio...  260 us
    reduce_scatter x1, waiting for transfers between devices, on_device(): lax.psum_scatter(attn_part.astype(jnp.bfloat16), 'heads', scatter_dimensi...  252 us
    all_to_all x1, blocking collectives, on_device(): lax.all_to_all(jnp.stack([normed] * lax.axis_size('heads')), 'heads', 0, 0)  64.9 us
    reduce_scatter x1, waiting for transfers between devices, on_device(): lax.psum_scatter(up_part, 'width', scatter_dimension=0, tiled=True)  51.4 us
    reduce_scatter x1, waiting for transfers between devices, on_device(): lax.psum_scatter(qkv_part, 'width', scatter_dimension=0, tiled=True)  49.9 us
    all_gather x1, blocking collectives, on_device(): value_rows = lax.all_gather(value_cache, 'width', axis=0, tiled=True)  19 us
    psum x1, blocking collectives, on_device(): lax.psum((jnp.sum(floats, -1), jnp.sum(floats * floats, -1)), 'width')  17.6 us
    all_gather x1, blocking collectives, on_device(): key_rows = lax.all_gather(key_cache, 'width', axis=0, tiled=True)  16.9 us
  transfers between devices with their start and end apart: 5, of which 4 were waited for; matrix products, arithmetic and copies ran while one was open for 3% of the time, Pallas kernels for 0%

profile of v1, /device:TPU:2, one launch (start us, length us, event | category | flops | bytes accessed | tf_op | source)
XLA Modules:
  0.0 797.8 jit_solution(13250024622613973606)
XLA Ops:
  7.2 1.1 convert_reduce_fusion
  8.3 17.6 %all-reduce = (f32[48]{0:T(128)S(1)}, f32[48]{0:T(128)S(1)}) all-reduce(f32[48]{0:T(128)S(1)} %get-tuple-element.13, f32[48]{0:T(128)S(1)} %get-tuple-element.12), channel_id=1, replica_groups=mesh['heads'=32,'width'=8] {'width'}, use_global_device_ids=true, to_apply=%region_3.0 | all-reduce | flops 96 | bytes 768 | tf_op jit(solution)/shard_map/psum | solution.py:55
  26.0 1.0 fusion.41
  27.0 0.2 stack.2
  27.1 64.9 %all_to_all.5 = bf16[32,48,768]{2,1,0:T(8,128)(2,1)S(1)} all-to-all(bf16[32,48,768]{2,1,0:T(8,128)(2,1)S(1)} %stack.2), channel_id=1, replica_groups=mesh['heads'=32,'width'=8] {'heads'}, dimensions={0} | all-to-all | bytes 4718592 | tf_op jit(solution)/shard_map/all_to_all | solution.py:62
  92.1 4.2 fusion.5
  96.3 0.6 copy-done.13
  96.9 5.1 fusion.7
  102.1 0.6 copy-done.5
  103.0 0.3 reduce-window.9
  103.5 51.4 %reduce-scatter.9.cloned.1.call-done = f32[192,768]{1,0:T(8,128)} async-done(((f32[1536,768]{1,0:T(8,128)}), f32[192,768]{1,0:T(8,128)}) %reduce-scatter.9.cloned.1.call-update) | async-done | bytes 589840 | tf_op jit(solution)/shard_map/reduce_scatter | solution.py:85
  154.9 3.1 fusion.32
  158.6 0.5 fusion.19
  159.1 49.9 %reduce-scatter.5.cloned.1.call-done = f32[192,576]{1,0:T(8,128)} async-done(((f32[1536,576]{1,0:T(8,128)}), f32[192,576]{1,0:T(8,128)}) %reduce-scatter.5.cloned.1.call-update) | async-done | bytes 442384 | tf_op jit(solution)/shard_map/reduce_scatter | solution.py:84
  209.0 1.1 broadcast_add_fusion
  210.0 0.2 copy.38
  210.5 0.8 copy.46
  211.5 0.8 subtract_convert_fusion.1
  212.7 16.9 %all_gather.12 = bf16[1536,192]{1,0:T(8,128)(2,1)S(1)} all-gather(bf16[192,192]{1,0:T(8,128)(2,1)S(1)} %copy.44), channel_id=1, replica_groups=mesh['heads'=32,'width'=8] {'width'}, dimensions={0}, use_global_device_ids=true | all-gather | bytes 663552 | tf_op jit(solution)/shard_map/all_gather | solution.py:95
  229.6 0.3 copy.45
  229.9 19.0 %all_gather.13 = bf16[1536,192]{1,0:T(8,128)(2,1)S(1)} all-gather(bf16[192,192]{1,0:T(8,128)(2,1)S(1)} %copy-done.2), channel_id=1, replica_groups=mesh['heads'=32,'width'=8] {'width'}, dimensions={0}, use_global_device_ids=true | all-gather | bytes 663552 | tf_op jit(solution)/shard_map/all_gather | solution.py:96
  248.9 0.3 copy.47
  249.1 1.7 fusion.55
  250.9 0.7 fusion.13
  251.6 0.7 fusion.27
  252.4 15.9 %all_gather.14 = bf16[1536,192]{1,0:T(8,128)(2,1)S(1)} all-gather(bf16[192,192]{1,0:T(8,128)(2,1)S(1)} %copy.48), channel_id=1, replica_groups=mesh['heads'=32,'width'=8] {'width'}, dimensions={0}, use_global_device_ids=true | all-gather | bytes 663552 | tf_op jit(solution)/shard_map/all_gather | solution.py:125
  268.3 2.2 convolution_convert_fusion.1
  270.6 1.2 copy-done.10
  271.8 5.1 convolution_convert_fusion
  276.9 252.3 %reduce-scatter.7.cloned.1.call-done = bf16[48,768]{1,0:T(8,128)(2,1)} async-done(((bf16[1536,768]{1,0:T(8,128)(2,1)}), bf16[48,768]{1,0:T(8,128)(2,1)}) %reduce-scatter.7.cloned.1.call-update) | async-done | bytes 73744 | tf_op jit(solution)/shard_map/reduce_scatter | solution.py:135
  529.2 260.5 %reduce-scatter.11.cloned.1.call-done = bf16[48,768]{1,0:T(8,128)(2,1)} async-done(((bf16[1536,768]{1,0:T(8,128)(2,1)}), bf16[48,768]{1,0:T(8,128)(2,1)}) %reduce-scatter.11.cloned.1.call-update) | async-done | bytes 73744 | tf_op jit(solution)/shard_map/reduce_scatter | solution.py:137
  789.7 1.6 fusion.45
  (63 shorter events, 2.3 us)
Async XLA Ops:
  7.2 84.9 %copy-start = (bf16[768,768]{1,0:T(8,128)(2,1)S(1)}, bf16[768,768]{1,0:T(8,128)(2,1)}, u32[]{:S(2)}) copy-start(bf16[768,768]{1,0:T(8,128)(2,1)} %param.24) | copy-start | bytes 3538948
  7.2 147.7 %reduce-scatter.9.cloned.1.call-start = ((), (), s32[]{:S(2)}) async-start(), calls=%async_computation.7 | async-start | bytes 5308416 | tf_op jit(solution)/shard_map/reduce_scatter | solution.py:85
  27.1 64.9 %copy-start.11 = (f32[768]{0:T(1024)S(1)}, f32[768]{0:T(1024)}, u32[]{:S(2)}) copy-start(f32[768]{0:T(1024)} %param.19) | copy-start | bytes 9220
  27.1 64.9 %copy-start.12 = (f32[768]{0:T(1024)S(1)}, f32[768]{0:T(1024)}, u32[]{:S(2)}) copy-start(f32[768]{0:T(1024)} %param.18) | copy-start | bytes 9220
  96.2 0.7 copy-start.13
  96.2 0.7 copy-start.14
  96.2 112.7 %reduce-scatter.5.cloned.1.call-start = ((), (), s32[]{:S(2)}) async-start(), calls=%async_computation.5 | async-start | bytes 4423680 | tf_op jit(solution)/shard_map/reduce_scatter | solution.py:84
  102.0 0.7 copy-start.5
  102.0 52.9 %copy-start.6 = (f32[768]{0:T(1024)S(1)}, f32[768]{0:T(1024)}, u32[]{:S(2)}) copy-start(f32[768]{0:T(1024)} %param.25) | copy-start | bytes 9220
  102.0 106.9 %copy-start.7 = (f32[576]{0:T(1024)S(1)}, f32[576]{0:T(1024)}, u32[]{:S(2)}) copy-start(f32[576]{0:T(1024)} %param.21) | copy-start | bytes 6916
  102.1 168.5 %all-gather.2.cloned.1.call-start = ((), (), s32[]{:S(2)}) async-start(), calls=%async_computation.8 | async-start | bytes 2654208 | tf_op jit(solution)/shard_map/all_gather | solution.py:131
  158.0 371.2 %reduce-scatter.7.cloned.1.call-start = ((), (), s32[]{:S(2)}) async-start(), calls=%async_computation.6 | async-start | bytes 2433024 | tf_op jit(solution)/shard_map/reduce_scatter | solution.py:135
  211.4 18.5 %copy-start.2 = (bf16[192,192]{1,0:T(8,128)(2,1)S(1)}, bf16[192,192]{1,0:T(8,128)(2,1)}, u32[]{:S(2)}) copy-start(bf16[192,192]{1,0:T(8,128)(2,1)} %copy.46) | copy-start | bytes 221188
  212.7 17.2 %copy-start.3 = (bf16[192,192]{1,0:T(8,128)(2,1)}, bf16[192,192]{1,0:T(8,128)(2,1)S(1)}, u32[]{:S(2)}) copy-start(bf16[192,192]{1,0:T(8,128)(2,1)S(1)} %copy.44) | copy-start | bytes 221188
  251.6 16.7 %copy-start.4 = (bf16[192,768]{1,0:T(8,128)(2,1)S(1)}, bf16[192,768]{1,0:T(8,128)(2,1)}, u32[]{:S(2)}) copy-start(bf16[192,768]{1,0:T(8,128)(2,1)} %param.22) | copy-start | bytes 884740
  270.5 1.3 copy-start.10
  270.5 519.1 %reduce-scatter.11.cloned.1.call-start = ((), (), s32[]{:S(2)}) async-start(), calls=%async_computation.9 | async-start | bytes 2433024 | tf_op jit(solution)/shard_map/reduce_scatter | solution.py:137
  276.9 512.8 %copy-start.1 = (bf16[48,768]{1,0:T(8,128)(2,1)S(1)}, bf16[48,768]{1,0:T(8,128)(2,1)}, u32[]{:S(2)}) copy-start(bf16[48,768]{1,0:T(8,128)(2,1)} %param.14) | copy-start | bytes 221188
  276.9 512.8 %copy-start.8 = (f32[768]{0:T(1024)S(1)}, f32[768]{0:T(1024)}, u32[]{:S(2)}) copy-start(f32[768]{0:T(1024)} %param.27) | copy-start | bytes 9220
  276.9 512.8 %copy-start.9 = (f32[768]{0:T(1024)S(1)}, f32[768]{0:T(1024)}, u32[]{:S(2)}) copy-start(f32[768]{0:T(1024)} %param.23) | copy-start | bytes 9220
Sparse Core Ops, SparseCore 0:
  96.4 58.5 reduce-scatter.8
  157.5 51.4 reduce-scatter.4
  210.8 44.6 all-gather.1
  270.6 258.5 reduce-scatter.6
  534.4 255.1 reduce-scatter.10
